TPU v7x, 32 devices: a whole 2x2x4 slice. The times are simulated.
32 devices in a mesh: row: 8 (over z, y), col: 4 (over x, core).
Axes of the slice: x: 2, y: 2, z: 4, core: 2. Of those that a mesh axis runs over, the one named last changes fastest.
Arguments:
- factor: float32 [4, 8, 256, 1024], P(None, 'row', None, 'col'), may hold values from -0.1875 to 0.1875
- rhs: float32 [4, 8, 256, 4096], P(None, 'row', None, 'col'), may hold values from -6 to 6
- diag_inv: float32 [4, 256, 256], replicated, may hold values from -0.5 to 1.3, as said below
Outputs:
- updated: float32 [4, 8, 256, 4096], P(None, 'row', None, 'col')
Inputs may be any that keep to these rules, and one draw needn't show every extreme that they name: Each diag_inv[k] is lower triangular with its diagonal between 0.7 and 1.3.
All inputs are finite; a program needn't handle non-finite values.
Results may differ from a plain program's by a relative error of at most 0.0001.
Values sent between devices are 32-bit elements; how exact they have to be, the bound alone decides.
No kernel may reach another device: no remote copies, remote signals or barrier semaphores. Data moves between devices by JAX's collectives and lax.ppermute only.
A program may use at most 64 MiB of HBM per device.

v0:
```python
import jax
import jax.numpy as jnp
from jax import lax
from jax.sharding import PartitionSpec as P

STEPS = 4


def broadcast(block, axis, holder):
    block = jnp.where(lax.axis_index(axis) == holder, block, jnp.zeros_like(block))
    return lax.psum(block, axis)


def matmul(left, right):
    return jnp.dot(left, right, precision=lax.Precision.HIGHEST, preferred_element_type=jnp.float32)


def per_device(factor, rhs, diag_inv):
    row_count = lax.axis_size("row")
    block_size = rhs.shape[2]
    local_blocks = rhs.shape[0]
    panel = lax.all_gather(factor, "col", axis=3, tiled=True)
    flat_panel = panel.reshape(local_blocks * block_size, STEPS * block_size)
    position = lax.axis_index("row")
    blocks = (jnp.arange(local_blocks, dtype=jnp.int32) * row_count + position)[:, None, None, None]
    work = rhs
    for step in range(STEPS):
        candidate = matmul(diag_inv[step], work[0, 0])
        solved = broadcast(candidate, "row", step)
        update = matmul(flat_panel[:, step * block_size : (step + 1) * block_size], solved).reshape(
            work.shape
        )
        work = jnp.where(
            blocks > step, work - update, jnp.where(blocks == step, solved[None, None], work)
        )
    return work


def solution(mesh):
    return jax.shard_map(
        per_device,
        mesh=mesh,
        in_specs=(P(None, "row", None, "col"), P(None, "row", None, "col"), P()),
        out_specs=P(None, "row", None, "col"),
        check_vma=False,
    )
```

profile of v0, /device:TPU:24, one launch (start us, length us, event | category | flops | bytes accessed | tf_op | source)
XLA Modules:
  0.0 391.7 jit_solution(5680344564141285933)
XLA Ops:
  7.4 0.0 all-reduce.5.cloned.1.call-start
  7.4 3.3 convolution_select_fusion.3
  10.7 0.0 all-reduce.5.cloned.1.call-update
  10.7 0.0 all-gather.2.cloned.1.call-start
  10.8 0.5 all-gather.2.cloned.1.call-update
  11.3 0.0 all-reduce.7.cloned.1.call-start
  11.4 78.4 %all-reduce.5.cloned.1.call-done = f32[256,1024]{1,0:T(8,128)} async-done(((f32[256,1024]{1,0:T(8,128)}), f32[256,1024]{1,0:T(8,128)}) %all-reduce.5.cloned.1.call-update) | async-done | bytes 1048592 | tf_op jit(solution)/shard_map/psum | solution.py:11
  89.8 0.0 copy-start.7
  89.8 0.0 all-gather.2.cloned.1.call-done
  89.8 0.0 copy-start.3
  89.8 5.4 %fusion.9 = f32[1024,1024]{0,1:T(8,128)S(1)} fusion(f32[256,1024]{1,0:T(8,128)} %all-reduce.5.cloned.1.call-done, f32[1024,1024]{1,0:T(8,128)} %bitcast.59), kind=kOutput, calls=%fused_computation.20 | convolution fusion | flops 3221225472 | bytes 6291456 | tf_op jit(solution)/shard_map/dot_general | solution.py:15
  95.2 0.0 copy-done.7
  95.2 0.0 copy-done.3
  95.2 0.0 copy-start.8
  95.2 1.6 select_select_fusion.3
  96.8 0.0 copy-start.1
  96.8 2.0 copy-done.1
  98.8 0.0 copy-done.8
  98.8 2.8 fusion.2
  101.7 0.0 all-reduce.7.cloned.1.call-update
  101.7 0.2 all-reduce.9.cloned.1.call-start
  102.0 77.8 %all-reduce.7.cloned.1.call-done = f32[256,1024]{0,1:T(8,128)} async-done(((f32[256,1024]{0,1:T(8,128)}), f32[256,1024]{0,1:T(8,128)}) %all-reduce.7.cloned.1.call-update) | async-done | bytes 1048592 | tf_op jit(solution)/shard_map/psum | solution.py:11
  179.7 0.0 copy-start.4
  179.7 7.1 %fusion.7 = f32[1024,1024]{0,1:T(8,128)} fusion(f32[256,1024]{0,1:T(8,128)} %all-reduce.7.cloned.1.call-done, f32[1024,1024]{1,0:T(8,128)} %bitcast.60), kind=kOutput, calls=%fused_computation.17 | convolution fusion | flops 3221225472 | bytes 6291456 | tf_op jit(solution)/shard_map/dot_general | solution.py:15
  186.8 0.0 copy-done.4
  186.8 0.3 copy.6
  187.2 4.7 %select_select_fusion.2 = f32[4,1,256,1024]{3,2,1,0:T(8,128)S(1)} fusion(f32[4,1,256,1024]{3,2,1,0:T(8,128)} %copy-done.1, f32[4,1,256,1024]{3,2,1,0:T(8,128)} %bitcast.56, f32[256,1024]{1,0:T(8,128)S(1)} %copy.6, pred[4]{0:T(512)(128)(4,1)S(1)} %get-tuple-element.7, pred[4]{0:T(512)(128)(4,1)S(1)} %get-tuple-element.8), kind=kLoop, calls=%fused_computation.2 | loop fusion | flops 3145728 | bytes 13631496 | tf_op jit(solution)/shard_map/jit(_where)/select_n | solution.py:33
  191.9 0.0 copy-start
  191.9 2.0 copy-done
  193.9 2.8 fusion.1
  196.8 0.0 all-reduce.9.cloned.1.call-update
  196.8 0.3 all-reduce.11.cloned.1.call-start
  197.1 77.8 %all-reduce.9.cloned.1.call-done = f32[256,1024]{0,1:T(8,128)} async-done(((f32[256,1024]{0,1:T(8,128)}), f32[256,1024]{0,1:T(8,128)}) %all-reduce.9.cloned.1.call-update) | async-done | bytes 1048592 | tf_op jit(solution)/shard_map/psum | solution.py:11
  274.9 0.0 copy-start.5
  274.9 7.1 %fusion.5 = f32[1024,1024]{0,1:T(8,128)} fusion(f32[256,1024]{0,1:T(8,128)} %all-reduce.9.cloned.1.call-done, f32[1024,1024]{1,0:T(8,128)} %bitcast.61), kind=kOutput, calls=%fused_computation.14 | convolution fusion | flops 3221225472 | bytes 6291456 | tf_op jit(solution)/shard_map/dot_general | solution.py:15
  282.0 0.0 copy-done.5
  282.0 0.3 copy.8
  282.4 4.7 %select_select_fusion.1 = f32[4,1,256,1024]{3,2,1,0:T(8,128)S(1)} fusion(f32[4,1,256,1024]{3,2,1,0:T(8,128)} %copy-done, f32[4,1,256,1024]{3,2,1,0:T(8,128)} %bitcast.57, f32[256,1024]{1,0:T(8,128)S(1)} %copy.8, pred[4]{0:T(512)(128)(4,1)S(1)} %get-tuple-element.9, pred[4]{0:T(512)(128)(4,1)S(1)} %get-tuple-element.10), kind=kLoop, calls=%fused_computation.1 | loop fusion | flops 3145728 | bytes 13631496 | tf_op jit(solution)/shard_map/jit(_where)/select_n | solution.py:33
  287.1 0.0 copy-start.2
  287.1 2.0 copy-done.2
  289.1 2.8 fusion
  292.0 0.0 all-reduce.11.cloned.1.call-update
  292.0 78.0 %all-reduce.11.cloned.1.call-done = f32[256,1024]{0,1:T(8,128)} async-done(((f32[256,1024]{0,1:T(8,128)}), f32[256,1024]{0,1:T(8,128)}) %all-reduce.11.cloned.1.call-update) | async-done | bytes 1048592 | tf_op jit(solution)/shard_map/psum | solution.py:11
  370.0 0.0 copy-start.6
  370.0 7.1 %fusion.3 = f32[1024,1024]{0,1:T(8,128)} fusion(f32[256,1024]{0,1:T(8,128)} %all-reduce.11.cloned.1.call-done, f32[1024,1024]{1,0:T(8,128)} %bitcast.62), kind=kOutput, calls=%fused_computation.11 | convolution fusion | flops 3221225472 | bytes 6291456 | tf_op jit(solution)/shard_map/dot_general | solution.py:15
  377.1 0.0 copy-done.6
  377.1 0.3 copy.10
  377.5 7.1 %select_select_fusion = f32[4,1,256,1024]{3,2,1,0:T(8,128)} fusion(f32[4,1,256,1024]{3,2,1,0:T(8,128)} %copy-done.2, f32[4,1,256,1024]{3,2,1,0:T(8,128)} %bitcast.55, f32[256,1024]{1,0:T(8,128)S(1)} %copy.10, pred[4]{0:T(512)(128)(4,1)S(1)} %get-tuple-element.11, pred[4]{0:T(512)(128)(4,1)S(1)} %get-tuple-element.12), kind=kLoop, calls=%fused_computation | loop fusion | flops 3145728 | bytes 13631496 | tf_op jit(solution)/shard_map/jit(_where)/select_n | solution.py:33
  (4 shorter events, 0.0 us)
Async XLA Ops:
  7.4 82.4 %all-reduce.5.cloned.1.call-start = ((), (), s32[]{:S(2)}) async-start(), calls=%async_computation | async-start | bytes 2097152 | tf_op jit(solution)/shard_map/psum | solution.py:11
  10.7 79.0 %all-gather.2.cloned.1.call-start = ((), (), s32[]{:S(2)}) async-start(), calls=%async_computation.1 | async-start | bytes 5242880 | tf_op jit(solution)/shard_map/all_gather | solution.py:22
  11.3 168.4 %all-reduce.7.cloned.1.call-start = ((), (), s32[]{:S(2)}) async-start(), calls=%async_computation.2 | async-start | bytes 2097152 | tf_op jit(solution)/shard_map/psum | solution.py:11
  89.8 5.4 %copy-start.7 = (f32[256,1024]{1,0:T(8,128)S(1)}, f32[256,1024]{1,0:T(8,128)}, u32[]{:S(2)}) copy-start(f32[256,1024]{1,0:T(8,128)} %all-reduce.5.cloned.1.call-done) | copy-start | bytes 3145732
  89.8 5.4 %copy-start.3 = (f32[4,1,256,1024]{3,2,1,0:T(8,128)S(1)}, f32[4,1,256,1024]{3,2,1,0:T(8,128)}, u32[]{:S(2)}) copy-start(f32[4,1,256,1024]{3,2,1,0:T(8,128)} %param.4) | copy-start | bytes 12582916
  95.2 3.7 copy-start.8
  96.8 2.0 copy-start.1
  101.7 173.2 %all-reduce.9.cloned.1.call-start = ((), (), s32[]{:S(2)}) async-start(), calls=%async_computation.3 | async-start | bytes 2097152 | tf_op jit(solution)/shard_map/psum | solution.py:11
  179.7 7.1 %copy-start.4 = (f32[256,1024]{0,1:T(8,128)S(1)}, f32[256,1024]{0,1:T(8,128)}, u32[]{:S(2)}) copy-start(f32[256,1024]{0,1:T(8,128)} %all-reduce.7.cloned.1.call-done) | copy-start | bytes 3145732
  191.9 2.0 copy-start
  196.8 173.2 %all-reduce.11.cloned.1.call-start = ((), (), s32[]{:S(2)}) async-start(), calls=%async_computation.4 | async-start | bytes 2097152 | tf_op jit(solution)/shard_map/psum | solution.py:11
  274.9 7.1 %copy-start.5 = (f32[256,1024]{0,1:T(8,128)S(1)}, f32[256,1024]{0,1:T(8,128)}, u32[]{:S(2)}) copy-start(f32[256,1024]{0,1:T(8,128)} %all-reduce.9.cloned.1.call-done) | copy-start | bytes 3145732
  287.1 2.0 copy-start.2
  370.0 7.1 %copy-start.6 = (f32[256,1024]{0,1:T(8,128)S(1)}, f32[256,1024]{0,1:T(8,128)}, u32[]{:S(2)}) copy-start(f32[256,1024]{0,1:T(8,128)} %all-reduce.11.cloned.1.call-done) | copy-start | bytes 3145732
Sparse Core Ops, SparseCore 0:
  11.7 78.0 all-reduce.4
  101.8 77.8 all-reduce.6
  196.9 77.9 all-reduce.8
  292.1 77.8 all-reduce.10
Sparse Core Ops, SparseCore 1:
  12.8 35.3 all-gather.1
where the time goes:
time: 395 us; the launch traced here: 392 us
  waiting for transfers between devices  313 us (79%)
  matrix products  38.6 us (10%)
  other arithmetic  18.2 us (5%)
  between operations  14.7 us (4%)
  local copies, waits for them, and re-layouts  7.04 us (2%)
    psum x4, waiting for transfers between devices, broadcast(): return lax.psum(block, axis)  312 us
    dot_general x8, matrix products, matmul(): jnp.dot(left, right, precision=lax.Precision.HIGHEST, preferred_element_t...  38.6 us
    select_n x4, other arithmetic, per_device(): jnp.where(blocks > step, work - update, jnp.where(blocks == step, solved[...  18.1 us
  transfers between devices with their start and end apart: 5, of which 4 were waited for; matrix products, arithmetic and copies ran while one was open for 0% of the time, Pallas kernels for 0%

commit v1 on v0

v1 whole, which is shorter than its diff:
```python
import jax
import jax.numpy as jnp
from jax import lax
from jax.sharding import PartitionSpec as P


def matmul(left, right):
    return jnp.dot(left, right, precision=lax.Precision.HIGHEST, preferred_element_type=jnp.float32)


def neighbours(n):
    kinds = [lambda u: u ^ 1, lambda u: u + 2, lambda u: u - 2]
    if n > 8:
        kinds += [lambda u: u + 8, lambda u: u - 8]
    return kinds


def schedule(n, sources):
    have = [set() for _ in range(n)]
    for item, row in sources.items():
        have[row].add(item)
    slots = []
    while any(len(h) < len(sources) for h in have):
        slot, incoming = [], [set() for _ in range(n)]
        for kind in neighbours(n):
            moves = []
            for u in range(n):
                v = kind(u)
                if not 0 <= v < n:
                    continue
                want = sorted(have[u] - have[v] - incoming[v])
                if want:
                    incoming[v].add(want[0])
                    moves.append((u, v, want[0]))
            if moves:
                slot.append(moves)
        for moves in slot:
            for u, v, item in moves:
                have[v].add(item)
        slots.append(slot)
    return slots


def broadcast(held, n, sources, trash):
    position = lax.axis_index("row")
    for slot in schedule(n, sources):
        received = []
        for moves in slot:
            send = [0] * n
            recv = [trash] * n
            for u, v, item in moves:
                send[u] = item
                recv[v] = item
            payload = held[jnp.asarray(send, jnp.int32)[position]]
            got = lax.ppermute(payload, "row", [(u, v) for u, v, _ in moves])
            received.append((jnp.asarray(recv, jnp.int32)[position], got))
        for index, got in received:
            held = lax.dynamic_update_index_in_dim(held, got, index, 0)
    return held


def per_device(factor, rhs, diag_inv):
    n = lax.axis_size("row")
    steps = diag_inv.shape[0]
    nb = rhs.shape[2]
    local_blocks = rhs.shape[0]
    position = lax.axis_index("row")

    held = jnp.zeros((steps + 1, nb, rhs.shape[3]), jnp.float32)
    held = lax.dynamic_update_index_in_dim(held, rhs[0, 0], jnp.minimum(position, steps), 0)
    held = broadcast(held, n, {k: k for k in range(steps)}, steps)

    panel = lax.all_gather(factor, "col", axis=3, tiled=True)

    width = (steps - 1) * nb
    top = jnp.zeros((steps + 1, nb, width), jnp.float32)
    top = lax.dynamic_update_index_in_dim(top, panel[0, 0, :, :width], jnp.minimum(position, steps), 0)
    top = broadcast(top, n, {k: k for k in range(1, steps)}, steps)

    solved = []
    for k in range(steps):
        acc = held[k]
        for j in range(k):
            acc = acc - matmul(top[k, :, j * nb : (j + 1) * nb], solved[j])
        solved.append(matmul(diag_inv[k], acc))
    every = jnp.concatenate(solved, axis=0)
    stacked = jnp.stack(solved)

    flat_panel = panel.reshape(local_blocks * nb, steps * nb)
    update = matmul(flat_panel, every).reshape(rhs.shape)
    work = rhs - update
    blocks = (jnp.arange(local_blocks, dtype=jnp.int32) * n + position)[:, None, None, None]
    mine = stacked[jnp.minimum(position, steps - 1)][None, None]
    return jnp.where(blocks < steps, mine, work)


def solution(mesh):
    return jax.shard_map(
        per_device,
        mesh=mesh,
        in_specs=(P(None, "row", None, "col"), P(None, "row", None, "col"), P()),
        out_specs=P(None, "row", None, "col"),
        check_vma=False,
    )
```

time: 395 us -> 265 us (0.67)
  waiting for transfers between devices: 313 us -> 82 us
  local copies, waits for them, and re-layouts: 7.04 us -> 61.9 us
  between operations: 14.7 us -> 55.1 us
  starting transfers between devices: 0.57 us -> 33.1 us
  other arithmetic: 18.2 us -> 3.7 us
  matrix products: 38.6 us -> 27.2 us
    psum x4 -> x0, waiting for transfers between devices: 312 us -> none  [broadcast(): return lax.psum(block, axis)]
    ppermute x0 -> x16, waiting for transfers between devices: none -> 72.9 us  [broadcast(): got = lax.ppermute(payload, 'row', [(u, v) for u, v, _ in moves])]
    ppermute x0 -> x16, starting transfers between devices: none -> 33.1 us  [broadcast(): got = lax.ppermute(payload, 'row', [(u, v) for u, v, _ in moves])]
    squeeze x0 -> x14, local copies, waits for them, and re-layouts: none -> 23.5 us  [broadcast(): payload = held[jnp.asarray(send, jnp.int32)[position]]]
    dynamic_update_slice x0 -> x12, local copies, waits for them, and re-layouts: none -> 17.4 us  [the longest x10 14.9 us: broadcast(): held = lax.dynamic_update_index_in_dim(held, got, index, 0)]
    select_n x4 -> x1, other arithmetic: 18.1 us -> 3.2 us  [per_device(): return jnp.where(blocks < steps, mine, work)]
    dynamic_slice x0 -> x22, local copies, waits for them, and re-layouts: none -> 13.9 us  [the longest x15 9.13 us: broadcast(): received.append((jnp.asarray(recv, jnp.int32)[position], got))]
    dot_general x8 -> x11, matrix products: 38.6 us -> 27.2 us  [matmul(): jnp.dot(left, right, precision=lax.Precision.HIGHEST, preferred_element_t...]
  transfers between devices with their start and end apart: 5 -> 17, of which waited for: 4 -> 7; matrix products, arithmetic and copies ran while one was open for 0% -> 21% of each run, Pallas kernels for 0% -> 0%
where the time goes in v1:
time: 265 us; the launch traced here: 263 us
  waiting for transfers between devices  82 us (31%)
  local copies, waits for them, and re-layouts  61.9 us (23%)
  between operations  55.1 us (21%)
  starting transfers between devices  33.1 us (12%)
  matrix products  27.2 us (10%)
  other arithmetic  3.7 us (1%)
    ppermute x16, waiting for transfers between devices, broadcast(): got = lax.ppermute(payload, 'row', [(u, v) for u, v, _ in moves])  72.9 us
    ppermute x16, starting transfers between devices, broadcast(): got = lax.ppermute(payload, 'row', [(u, v) for u, v, _ in moves])  33.1 us
    dot_general x11, matrix products, matmul(): jnp.dot(left, right, precision=lax.Precision.HIGHEST, preferred_element_t...  27.2 us
    squeeze x14, local copies, waits for them, and re-layouts, broadcast(): payload = held[jnp.asarray(send, jnp.int32)[position]]  23.5 us
    dynamic_update_slice x10, local copies, waits for them, and re-layouts, broadcast(): held = lax.dynamic_update_index_in_dim(held, got, index, 0)  14.9 us
    dynamic_slice x15, local copies, waits for them, and re-layouts, broadcast(): received.append((jnp.asarray(recv, jnp.int32)[position], got))  9.13 us
    all_gather x1, waiting for transfers between devices, per_device(): panel = lax.all_gather(factor, 'col', axis=3, tiled=True)  8.45 us
    unnamed x56, local copies, waits for them, and re-layouts  6.07 us
  transfers between devices with their start and end apart: 17, of which 7 were waited for; matrix products, arithmetic and copies ran while one was open for 21% of the time, Pallas kernels for 0%

profile of v1, /device:TPU:24, one launch (start us, length us, event | category | flops | bytes accessed | tf_op | source)
XLA Modules:
  0.0 263.0 jit_solution(13963368796416208630)
XLA Ops:
  6.5 0.7 all-gather.2.cloned.1.call-update
  7.3 1.2 dynamic_slice.147
  11.2 1.3 bitcast_dynamic-update-slice_fusion.8
  12.5 2.3 copy-done
  14.9 0.7 collective-permute-start
  15.6 1.6 collective-permute-start.1
  22.6 2.4 dynamic-slice_bitcast_fusion.5
  25.0 0.7 collective-permute-start.2
  33.6 2.3 bitcast_dynamic-update-slice_fusion.6
  35.9 8.5 %all-gather.2.cloned.1.call-done = f32[4,1,256,1024]{3,2,1,0:T(8,128)} async-done(((f32[4,1,256,256]{3,2,1,0:T(8,128)}), f32[4,1,256,1024]{3,2,1,0:T(8,128)}) %all-gather.2.cloned.1.call-update) | async-done | bytes 4194320 | tf_op jit(solution)/shard_map/all_gather | solution.py:73
  44.7 1.2 fusion.22
  45.9 1.9 copy-done.2
  47.9 1.6 collective-permute-start.8
  49.5 1.1 bitcast_dynamic-update-slice_fusion.5
  50.5 1.3 dynamic-slice_bitcast_fusion.4
  51.8 0.7 collective-permute-start.3
  55.0 1.6 collective-permute-start.9
  56.6 2.6 dynamic-slice_bitcast_fusion.12
  59.2 1.6 collective-permute-start.10
  68.2 2.4 dynamic-slice_bitcast_fusion.3
  70.6 1.3 collective-permute-start.4
  71.9 2.1 bitcast_dynamic-update-slice_fusion.15
  73.9 2.1 bitcast_dynamic-update-slice_fusion.14
  76.0 1.2 dynamic-slice_bitcast_fusion.11
  77.2 1.6 collective-permute-start.11
  86.1 19.4 %collective-permute-done.4 = f32[256,1024]{1,0:T(8,128)S(1)} collective-permute-done((f32[256,1024]{1,0:T(8,128)S(1)}, f32[256,1024]{1,0:T(8,128)S(1)}, u32[]{:S(2)}, u32[]{:S(2)}) %collective-permute-start.4) | collective-permute-done | bytes 1048608 | tf_op jit(solution)/shard_map/ppermute | solution.py:55
  105.6 1.0 bitcast_dynamic-update-slice_fusion.3
  106.6 2.6 dynamic-slice_bitcast_fusion.10
  109.2 1.3 collective-permute-start.12
  110.5 1.3 dynamic-slice_bitcast_fusion.2
  111.8 3.9 %collective-permute-start.5 = (f32[256,1024]{1,0:T(8,128)S(1)}, f32[256,1024]{1,0:T(8,128)S(1)}, u32[]{:S(2)}, u32[]{:S(2)}) collective-permute-start(f32[256,1024]{1,0:T(8,128)S(1)} %dynamic-slice_bitcast_fusion.2), channel_id=1, source_target_pairs={{16,20},{20,16},{24,28},{28,24},{17,21},{21,17},{25,29},{29,25},{1... | collective-permute-start | bytes 3145736 | tf_op jit(solution)/shard_map/ppermute | solution.py:55
  122.9 26.5 %collective-permute-done.12 = f32[256,768]{1,0:T(8,128)S(1)} collective-permute-done((f32[256,768]{1,0:T(8,128)}, f32[256,768]{1,0:T(8,128)S(1)}, u32[]{:S(2)}, u32[]{:S(2)}) %collective-permute-start.12) | collective-permute-done | bytes 786464 | tf_op jit(solution)/shard_map/ppermute | solution.py:55
  149.4 0.9 bitcast_dynamic-update-slice_fusion.12
  150.4 1.2 dynamic-slice_bitcast_fusion.9
  151.6 3.4 %collective-permute-start.13 = (f32[256,768]{1,0:T(8,128)S(1)}, f32[256,768]{1,0:T(8,128)}, u32[]{:S(2)}, u32[]{:S(2)}) collective-permute-start(f32[256,768]{1,0:T(8,128)S(1)} %dynamic-slice_bitcast_fusion.9), channel_id=1, source_target_pairs={{20,16},{24,28},{28,24},{21,17},{25,29},{29,25},{22,18},{26,30},{3... | collective-permute-start | bytes 2359304 | tf_op jit(solution)/shard_map/ppermute | solution.py:55
  155.0 2.3 dynamic-slice_bitcast_fusion.1
  157.4 1.4 collective-permute-start.6
  166.1 4.0 %collective-permute-done.13 = f32[256,768]{1,0:T(8,128)} collective-permute-done((f32[256,768]{1,0:T(8,128)S(1)}, f32[256,768]{1,0:T(8,128)}, u32[]{:S(2)}, u32[]{:S(2)}) %collective-permute-start.13) | collective-permute-done | bytes 786464 | tf_op jit(solution)/shard_map/ppermute | solution.py:55
  170.1 2.6 dynamic-slice_bitcast_fusion.8
  172.7 1.7 collective-permute-start.14
  174.4 9.5 %collective-permute-done.6 = f32[256,1024]{1,0:T(8,128)S(1)} collective-permute-done((f32[256,1024]{1,0:T(8,128)S(1)}, f32[256,1024]{1,0:T(8,128)S(1)}, u32[]{:S(2)}, u32[]{:S(2)}) %collective-permute-start.6) | collective-permute-done | bytes 1048608 | tf_op jit(solution)/shard_map/ppermute | solution.py:55
  183.9 1.1 bitcast_dynamic-update-slice_fusion.1
  185.0 1.4 dynamic-slice_bitcast_fusion
  186.4 8.7 %collective-permute-start.7 = (f32[256,1024]{1,0:T(8,128)S(1)}, f32[256,1024]{1,0:T(8,128)S(1)}, u32[]{:S(2)}, u32[]{:S(2)}) collective-permute-start(f32[256,1024]{1,0:T(8,128)S(1)} %dynamic-slice_bitcast_fusion), channel_id=1, source_target_pairs={{24,28},{28,24},{25,29},{29,25},{26,30},{30,26},{27,31},{31,27}} | collective-permute-start | bytes 3145736 | tf_op jit(solution)/shard_map/ppermute | solution.py:55
  197.3 2.1 bitcast_dynamic-update-slice_fusion.10
  199.4 2.1 dynamic-slice_bitcast_fusion.7
  201.5 1.5 collective-permute-start.15
  207.8 4.7 %collective-permute-done.7 = f32[256,1024]{1,0:T(8,128)S(1)} collective-permute-done((f32[256,1024]{1,0:T(8,128)S(1)}, f32[256,1024]{1,0:T(8,128)S(1)}, u32[]{:S(2)}, u32[]{:S(2)}) %collective-permute-start.7) | collective-permute-done | bytes 1048608 | tf_op jit(solution)/shard_map/ppermute | solution.py:55
  212.5 1.1 bitcast_dynamic-update-slice_fusion
  213.5 2.5 fusion.21
  216.0 8.8 %collective-permute-done.15 = f32[256,768]{1,0:T(8,128)} collective-permute-done((f32[256,768]{1,0:T(8,128)}, f32[256,768]{1,0:T(8,128)}, u32[]{:S(2)}, u32[]{:S(2)}) %collective-permute-start.15) | collective-permute-done | bytes 786464 | tf_op jit(solution)/shard_map/ppermute | solution.py:55
  224.7 1.2 bitcast_dynamic-update-slice_fusion.9
  225.9 1.0 fusion.27
  227.0 1.0 fusion.26
  228.0 1.1 fusion.19
  229.2 1.0 fusion.25
  230.2 1.0 fusion.23
  231.2 1.0 fusion.24
  232.3 1.2 fusion.16
  233.5 1.2 convolution_subtract_fusion
  234.7 1.1 fusion.28
  235.8 14.9 %fusion = f32[1024,1024]{0,1:T(8,128)S(1)} fusion(f32[1024,1024]{1,0:T(8,128)S(1)} %bitcast.178, f32[256,1024]{1,0:T(8,128)S(1)} %bitcast.175, f32[256,1024]{1,0:T(8,128)S(1)} %bitcast.173, f32[256,1024]{1,0:T(8,128)S(1)} %bitcast.171, f32[256,1024]{1,0:T(8,128)S(1)} %bitcast.169), kind=kOutput, calls=%fused_computation.4 | convolution fusion | flops 12888047616 | bytes 12582912 | tf_op jit(solution)/shard_map/dot_general | solution.py:8
  251.3 1.7 copy-done.4
  252.9 3.2 %subtract_select_fusion = f32[4,1,256,1024]{3,2,1,0:T(8,128)} fusion(f32[4,1,256,1024]{3,2,1,0:T(8,128)S(1)} %copy-done.4, f32[4,1,256,1024]{3,2,1,0:T(8,128)S(1)} %bitcast.177, f32[256,1024]{1,0:T(8,128)S(1)} %fusion.11, pred[4]{0:T(512)(128)(4,1)S(1)} %add_compare_fusion), kind=kLoop, calls=%fused_computation.12 | loop fusion | flops 2097152 | bytes 13631492 | tf_op jit(solution)/shard_map/jit(_where)/select_n | solution.py:94
  (91 shorter events, 14.5 us)
Async XLA Ops:
  6.5 37.8 %all-gather.2.cloned.1.call-start = ((), (), s32[]{:S(2)}) async-start(), calls=%async_computation | async-start | bytes 5242880 | tf_op jit(solution)/shard_map/all_gather | solution.py:73
  10.5 6.8 %copy-start.27 = (s32[8]{0:T(128)S(1)}, s32[8]{0:T(128)}, u32[]{:S(2)}) copy-start(s32[8]{0:T(128)} %constant.108.clone) | copy-start | bytes 100
  10.5 8.7 %copy-start.26 = (s32[8]{0:T(128)S(1)}, s32[8]{0:T(128)}, u32[]{:S(2)}) copy-start(s32[8]{0:T(128)} %constant.106.clone) | copy-start | bytes 100
  11.1 14.6 %copy-start.25 = (s32[8]{0:T(128)S(1)}, s32[8]{0:T(128)}, u32[]{:S(2)}) copy-start(s32[8]{0:T(128)} %constant.107.clone) | copy-start | bytes 100
  11.1 16.5 %copy-start.24 = (s32[8]{0:T(128)S(1)}, s32[8]{0:T(128)}, u32[]{:S(2)}) copy-start(s32[8]{0:T(128)} %constant.109.clone) | copy-start | bytes 100
  11.2 18.5 %copy-start.23 = (s32[8]{0:T(128)S(1)}, s32[8]{0:T(128)}, u32[]{:S(2)}) copy-start(s32[8]{0:T(128)} %constant.110.clone) | copy-start | bytes 100
  12.5 2.3 copy-start
  14.9 7.7 %collective-permute-start = (f32[256,1024]{1,0:T(8,128)S(1)}, f32[256,1024]{1,0:T(8,128)S(1)}, u32[]{:S(2)}, u32[]{:S(2)}) collective-permute-start(f32[256,1024]{1,0:T(8,128)S(1)} %dynamic-slice_bitcast_fusion.6), channel_id=1, source_target_pairs={{0,4},{4,0},{8,12},{12,8},{1,5},{5,1},{9,13},{13,9},{2,6},{6,2},{1... | collective-permute-start | bytes 3145736 | tf_op jit(solution)/shard_map/ppermute | solution.py:55
  15.6 17.9 %collective-permute-start.1 = (f32[256,1024]{1,0:T(8,128)S(1)}, f32[256,1024]{1,0:T(8,128)}, u32[]{:S(2)}, u32[]{:S(2)}) collective-permute-start(f32[256,1024]{1,0:T(8,128)S(1)} %dynamic-slice_bitcast_fusion.6), channel_id=1, source_target_pairs={{0,8},{4,12},{8,16},{12,20},{1,9},{5,13},{9,17},{13,21},{2,10},{6,... | collective-permute-start | bytes 3145736 | tf_op jit(solution)/shard_map/ppermute | solution.py:55
  25.0 24.5 %collective-permute-start.2 = (f32[256,1024]{1,0:T(8,128)S(1)}, f32[256,1024]{1,0:T(8,128)S(1)}, u32[]{:S(2)}, u32[]{:S(2)}) collective-permute-start(f32[256,1024]{1,0:T(8,128)S(1)} %get-tuple-element.9), channel_id=1, source_target_pairs={{8,0},{12,4},{9,1},{13,5},{10,2},{14,6},{11,3},{15,7}} | collective-permute-start | bytes 3145736 | tf_op jit(solution)/shard_map/ppermute | solution.py:55
  44.7 7.9 %copy-start.22 = (s32[8]{0:T(128)S(1)}, s32[8]{0:T(128)}, u32[]{:S(2)}) copy-start(s32[8]{0:T(128)} %constant.120.clone) | copy-start | bytes 100
  45.9 1.9 copy-start.2
  47.8 12.9 %copy-start.21 = (s32[8]{0:T(128)S(1)}, s32[8]{0:T(128)}, u32[]{:S(2)}) copy-start(s32[8]{0:T(128)} %constant.112.clone) | copy-start | bytes 100
  47.8 14.8 %copy-start.20 = (s32[8]{0:T(128)S(1)}, s32[8]{0:T(128)}, u32[]{:S(2)}) copy-start(s32[8]{0:T(128)} %constant.111.clone) | copy-start | bytes 100
  47.8 16.4 %copy-start.19 = (s32[8]{0:T(128)S(1)}, s32[8]{0:T(128)}, u32[]{:S(2)}) copy-start(s32[8]{0:T(128)} %constant.121.clone) | copy-start | bytes 100
  47.9 8.7 %collective-permute-start.8 = (f32[256,768]{1,0:T(8,128)S(1)}, f32[256,768]{1,0:T(8,128)}, u32[]{:S(2)}, u32[]{:S(2)}) collective-permute-start(f32[256,768]{1,0:T(8,128)S(1)} %dynamic-slice_bitcast_fusion.13), channel_id=1, source_target_pairs={{4,0},{8,12},{12,8},{5,1},{9,13},{13,9},{6,2},{10,14},{14,10},{7,3... | collective-permute-start | bytes 2359304 | tf_op jit(solution)/shard_map/ppermute | solution.py:55
  51.8 16.4 %collective-permute-start.3 = (f32[256,1024]{1,0:T(8,128)S(1)}, f32[256,1024]{1,0:T(8,128)S(1)}, u32[]{:S(2)}, u32[]{:S(2)}) collective-permute-start(f32[256,1024]{1,0:T(8,128)S(1)} %dynamic-slice_bitcast_fusion.4), channel_id=1, source_target_pairs={{0,4},{4,0},{8,12},{12,8},{16,20},{20,16},{1,5},{5,1},{9,13},{13,9... | collective-permute-start | bytes 3145736 | tf_op jit(solution)/shard_map/ppermute | solution.py:55
  55.0 16.8 %collective-permute-start.9 = (f32[256,768]{1,0:T(8,128)S(1)}, f32[256,768]{1,0:T(8,128)}, u32[]{:S(2)}, u32[]{:S(2)}) collective-permute-start(f32[256,768]{1,0:T(8,128)S(1)} %dynamic-slice_bitcast_fusion.13), channel_id=1, source_target_pairs={{4,12},{8,16},{12,20},{5,13},{9,17},{13,21},{6,14},{10,18},{14,22}... | collective-permute-start | bytes 2359304 | tf_op jit(solution)/shard_map/ppermute | solution.py:55
  59.2 14.8 %collective-permute-start.10 = (f32[256,768]{1,0:T(8,128)}, f32[256,768]{1,0:T(8,128)}, u32[]{:S(2)}, u32[]{:S(2)}) collective-permute-start(f32[256,768]{1,0:T(8,128)} %get-tuple-element.15), channel_id=1, source_target_pairs={{8,0},{12,4},{9,1},{13,5},{10,2},{14,6},{11,3},{15,7}} | collective-permute-start | bytes 2359304 | tf_op jit(solution)/shard_map/ppermute | solution.py:55
  68.2 10.7 %copy-start.18 = (s32[8]{0:T(128)S(1)}, s32[8]{0:T(128)}, u32[]{:S(2)}) copy-start(s32[8]{0:T(128)} %constant.113.clone) | copy-start | bytes 100
  68.2 12.5 %copy-start.17 = (s32[8]{0:T(128)S(1)}, s32[8]{0:T(128)}, u32[]{:S(2)}) copy-start(s32[8]{0:T(128)} %constant.114.clone) | copy-start | bytes 100
  68.2 14.2 %copy-start.16 = (s32[8]{0:T(128)S(1)}, s32[8]{0:T(128)}, u32[]{:S(2)}) copy-start(s32[8]{0:T(128)} %constant.122.clone) | copy-start | bytes 100
  70.6 35.0 %collective-permute-start.4 = (f32[256,1024]{1,0:T(8,128)S(1)}, f32[256,1024]{1,0:T(8,128)S(1)}, u32[]{:S(2)}, u32[]{:S(2)}) collective-permute-start(f32[256,1024]{1,0:T(8,128)S(1)} %get-tuple-element.7), channel_id=1, source_target_pairs={{8,16},{12,20},{16,24},{20,28},{9,17},{13,21},{17,25},{21,29},{10,... | collective-permute-start | bytes 3145736 | tf_op jit(solution)/shard_map/ppermute | solution.py:55
  76.0 39.7 %copy-start.15 = (s32[8]{0:T(128)S(1)}, s32[8]{0:T(128)}, u32[]{:S(2)}) copy-start(s32[8]{0:T(128)} %constant.116.clone) | copy-start | bytes 100
  76.0 41.6 %copy-start.14 = (s32[8]{0:T(128)S(1)}, s32[8]{0:T(128)}, u32[]{:S(2)}) copy-start(s32[8]{0:T(128)} %constant.115.clone) | copy-start | bytes 100
  76.0 43.2 %copy-start.13 = (s32[8]{0:T(128)S(1)}, s32[8]{0:T(128)}, u32[]{:S(2)}) copy-start(s32[8]{0:T(128)} %constant.123.clone) | copy-start | bytes 100
  77.2 29.4 %collective-permute-start.11 = (f32[256,768]{1,0:T(8,128)S(1)}, f32[256,768]{1,0:T(8,128)}, u32[]{:S(2)}, u32[]{:S(2)}) collective-permute-start(f32[256,768]{1,0:T(8,128)S(1)} %dynamic-slice_bitcast_fusion.11), channel_id=1, source_target_pairs={{0,4},{4,0},{12,8},{16,20},{20,16},{1,5},{5,1},{13,9},{17,21},{21,... | collective-permute-start | bytes 2359304 | tf_op jit(solution)/shard_map/ppermute | solution.py:55
  109.2 40.2 %collective-permute-start.12 = (f32[256,768]{1,0:T(8,128)}, f32[256,768]{1,0:T(8,128)S(1)}, u32[]{:S(2)}, u32[]{:S(2)}) collective-permute-start(f32[256,768]{1,0:T(8,128)} %get-tuple-element.13), channel_id=1, source_target_pairs={{12,20},{16,24},{20,28},{13,21},{17,25},{21,29},{14,22},{18,26},{2... | collective-permute-start | bytes 2359304 | tf_op jit(solution)/shard_map/ppermute | solution.py:55
  111.8 47.0 %copy-start.12 = (s32[8]{0:T(128)S(1)}, s32[8]{0:T(128)}, u32[]{:S(2)}) copy-start(s32[8]{0:T(128)} %constant.117.clone) | copy-start | bytes 100
  111.8 48.8 %copy-start.11 = (s32[8]{0:T(128)S(1)}, s32[8]{0:T(128)}, u32[]{:S(2)}) copy-start(s32[8]{0:T(128)} %constant.118.clone) | copy-start | bytes 100
  111.8 50.6 %copy-start.10 = (s32[8]{0:T(128)S(1)}, s32[8]{0:T(128)}, u32[]{:S(2)}) copy-start(s32[8]{0:T(128)} %constant.124.clone) | copy-start | bytes 100
  111.8 43.2 %collective-permute-start.5 = (f32[256,1024]{1,0:T(8,128)S(1)}, f32[256,1024]{1,0:T(8,128)S(1)}, u32[]{:S(2)}, u32[]{:S(2)}) collective-permute-start(f32[256,1024]{1,0:T(8,128)S(1)} %dynamic-slice_bitcast_fusion.2), channel_id=1, source_target_pairs={{16,20},{20,16},{24,28},{28,24},{17,21},{21,17},{25,29},{29,25},{1... | collective-permute-start | bytes 3145736 | tf_op jit(solution)/shard_map/ppermute | solution.py:55
  151.6 18.5 %collective-permute-start.13 = (f32[256,768]{1,0:T(8,128)S(1)}, f32[256,768]{1,0:T(8,128)}, u32[]{:S(2)}, u32[]{:S(2)}) collective-permute-start(f32[256,768]{1,0:T(8,128)S(1)} %dynamic-slice_bitcast_fusion.9), channel_id=1, source_target_pairs={{20,16},{24,28},{28,24},{21,17},{25,29},{29,25},{22,18},{26,30},{3... | collective-permute-start | bytes 2359304 | tf_op jit(solution)/shard_map/ppermute | solution.py:55
  157.3 37.7 %copy-start.9 = (s32[8]{0:T(128)S(1)}, s32[8]{0:T(128)}, u32[]{:S(2)}) copy-start(s32[8]{0:T(128)} %constant.125.clone) | copy-start | bytes 100
  157.4 26.5 %collective-permute-start.6 = (f32[256,1024]{1,0:T(8,128)S(1)}, f32[256,1024]{1,0:T(8,128)S(1)}, u32[]{:S(2)}, u32[]{:S(2)}) collective-permute-start(f32[256,1024]{1,0:T(8,128)S(1)} %get-tuple-element.5), channel_id=1, source_target_pairs={{16,24},{20,28},{17,25},{21,29},{18,26},{22,30},{19,27},{23,31}} | collective-permute-start | bytes 3145736 | tf_op jit(solution)/shard_map/ppermute | solution.py:55
  172.7 30.2 %copy-start.8 = (s32[8]{0:T(128)S(1)}, s32[8]{0:T(128)}, u32[]{:S(2)}) copy-start(s32[8]{0:T(128)} %constant.119.clone) | copy-start | bytes 100
  172.7 32.0 %copy-start.7 = (s32[8]{0:T(128)S(1)}, s32[8]{0:T(128)}, u32[]{:S(2)}) copy-start(s32[8]{0:T(128)} %constant.126.clone) | copy-start | bytes 100
  172.7 24.6 %collective-permute-start.14 = (f32[256,768]{1,0:T(8,128)}, f32[256,768]{1,0:T(8,128)}, u32[]{:S(2)}, u32[]{:S(2)}) collective-permute-start(f32[256,768]{1,0:T(8,128)} %get-tuple-element.11), channel_id=1, source_target_pairs={{20,28},{21,29},{22,30},{23,31}} | collective-permute-start | bytes 2359304 | tf_op jit(solution)/shard_map/ppermute | solution.py:55
  185.0 28.6 %copy-start.5 = (f32[4,256,256]{2,1,0:T(8,128)S(1)}, f32[4,256,256]{2,1,0:T(8,128)}, u32[]{:S(2)}) copy-start(f32[4,256,256]{2,1,0:T(8,128)} %param.37) | copy-start | bytes 3145732
  186.4 26.1 %collective-permute-start.7 = (f32[256,1024]{1,0:T(8,128)S(1)}, f32[256,1024]{1,0:T(8,128)S(1)}, u32[]{:S(2)}, u32[]{:S(2)}) collective-permute-start(f32[256,1024]{1,0:T(8,128)S(1)} %dynamic-slice_bitcast_fusion), channel_id=1, source_target_pairs={{24,28},{28,24},{25,29},{29,25},{26,30},{30,26},{27,31},{31,27}} | collective-permute-start | bytes 3145736 | tf_op jit(solution)/shard_map/ppermute | solution.py:55
  201.5 23.3 %collective-permute-start.15 = (f32[256,768]{1,0:T(8,128)}, f32[256,768]{1,0:T(8,128)}, u32[]{:S(2)}, u32[]{:S(2)}) collective-permute-start(f32[256,768]{1,0:T(8,128)} %dynamic-slice_bitcast_fusion.7), channel_id=1, source_target_pairs={{28,24},{29,25},{30,26},{31,27}} | collective-permute-start | bytes 2359304 | tf_op jit(solution)/shard_map/ppermute | solution.py:55
  207.8 17.0 %copy-start.3 = (f32[5,256,768]{2,1,0:T(8,128)S(1)}, f32[5,256,768]{2,1,0:T(8,128)}, u32[]{:S(2)}) copy-start(f32[5,256,768]{2,1,0:T(8,128)} %bitcast_dynamic-update-slice_fusion.10) | copy-start | bytes 11796484
  213.5 14.5 %copy-start.1 = (f32[5,256,1024]{2,1,0:T(8,128)S(1)}, f32[5,256,1024]{2,1,0:T(8,128)}, u32[]{:S(2)}) copy-start(f32[5,256,1024]{2,1,0:T(8,128)} %bitcast_dynamic-update-slice_fusion) | copy-start | bytes 15728644
  233.5 2.3 copy-start.6
  250.7 2.2 copy-start.4
Sparse Core Ops, SparseCore 0:
  8.9 35.4 all-gather.1
